TPU v7x, 256 devices: a whole 4x4x8 slice. The times are simulated.
256 devices in a mesh: section: 2 (over core), req: 32 (over z, y), head: 4 (over x).
Axes of the slice: x: 4, y: 4, z: 8, core: 2. Of those that a mesh axis runs over, the one named last changes fastest.
Arguments:
- token_ids: int32 [128, 4], P('req'), may hold values from 0 to 31999
- request_order: int32 [128], replicated, may hold values from 0 to 127, each once
- window_lengths: int32 [128], replicated, may hold values from 1 to 512, as said below
- embed_table: bfloat16 [32000, 2048], P(('req', 'head')), may hold values from -6 to 6
- cache_arrived: bfloat16 [2, 128, 512, 2, 2048], P('section', None, 'req', None, 'head'), may hold values from -16 to 16
- state_arrived: float32 [2, 128, 128, 16, 128], P('section', None, 'req', 'head'), may hold values from -2 to 2
- conv_history: bfloat16 [2, 128, 3, 3, 2048], P('section', 'req', None, None, 'head'), may hold values from -6 to 6
- sink_cache: bfloat16 [2, 128, 4, 2, 2048], P('section', 'req', None, None, 'head'), may hold values from -16 to 16
- w_qkv: bfloat16 [2, 2048, 3, 2048], P('section', None, None, 'head'), may hold values from -0.125 to 0.125
- w_out: bfloat16 [2, 2048, 2048], P('section', 'head'), may hold values from -0.125 to 0.125
- w_beta: bfloat16 [2, 2048, 16], P('section', None, 'head'), may hold values from -0.125 to 0.125
- conv_taps: float32 [2, 4, 3, 2048], P('section', None, None, 'head'), may hold values from -3 to 3
- pre_gain: float32 [2, 2048], P('section'), may hold values from 0.25 to 1.75
- out_gain: float32 [2, 2048], P('section', 'head'), may hold values from 0.25 to 1.75
- score_scale_table: float32 [2, 16], P('section', 'head'), may hold values from 4 to 512
Outputs:
- layer_out: bfloat16 [2, 128, 4, 2048], P('section', 'req')
- final_state: float32 [2, 128, 128, 16, 128], P('section', 'req', None, 'head')
Inputs may be any that keep to these rules, and one draw needn't show every extreme that they name: `request_order`: a permutation of the arriving requests. `window_lengths`: some request holds a full window.
All inputs are finite; a program needn't handle non-finite values.
Results may differ from a plain program's by a relative error of at most 0.025.
Values may be sent and summed in bfloat16 or wider, within the bound.
No kernel may reach another device: no remote copies, remote signals or barrier semaphores. Data moves between devices by JAX's collectives and lax.ppermute only.
A program may use at most 128 MiB of HBM per device.

v0:
```python
import jax
import jax.numpy as jnp
from jax import lax
from jax.sharding import PartitionSpec as P

WIN = 512
epsilon = 1e-06
negative_big = -1e30


def passed_along(value, axis, by):
    peers = lax.axis_size(axis)
    pairs = [(i, i + by) for i in range(peers) if 0 <= i + by < peers]
    return lax.ppermute(value, axis, pairs)


def rms_scale(values, gain_row):
    return (
        values * lax.rsqrt(jnp.mean(values * values, axis=-1, keepdims=True) + epsilon) * gain_row
    )


def unit_rows(values):
    return values * lax.rsqrt(jnp.sum(values * values, axis=-1, keepdims=True) + epsilon)


def shards(
    token_ids,
    request_order,
    window_lengths,
    embed_table,
    cache_arrived,
    state_arrived,
    conv_history,
    sink_cache,
    w_qkv,
    w_out,
    w_beta,
    conv_taps,
    pre_gain,
    out_gain,
    score_scale_table,
):
    slot_count, token_count = token_ids.shape
    heads_dev = score_scale_table.shape[1]
    width = pre_gain.shape[1]
    local_width = out_gain.shape[1]
    head_dim = local_width // heads_dev
    group_index = lax.axis_index("req")
    section_index = lax.axis_index("section")
    vocab_dev = embed_table.shape[0]
    all_ids = lax.all_gather(token_ids, "req", axis=0, tiled=True)
    first_row = lax.axis_index(("req", "head")) * vocab_dev
    onehot = (
        all_ids.reshape(-1)[:, None] == first_row + jnp.arange(vocab_dev, dtype=jnp.int32)[None, :]
    ).astype(jnp.bfloat16)
    looked_up = jnp.dot(onehot, embed_table, preferred_element_type=jnp.float32)
    summed = lax.psum(looked_up, ("req", "head"))
    own_rows = lax.dynamic_slice_in_dim(
        summed, group_index * slot_count * token_count, slot_count * token_count, 0
    )
    embedded = own_rows.astype(jnp.bfloat16).reshape(slot_count, token_count, width)
    ordered_states = jnp.take(state_arrived, request_order, axis=1)
    delta_state = lax.all_to_all(ordered_states, "req", split_axis=1, concat_axis=2, tiled=True)[0]
    ordered_cache = jnp.take(cache_arrived, request_order, axis=1)
    all_lengths = jnp.take(window_lengths, request_order)
    own_lengths = lax.dynamic_slice_in_dim(all_lengths, group_index * slot_count, slot_count, 0)
    window_cache = lax.all_to_all(ordered_cache, "req", split_axis=1, concat_axis=2, tiled=True)[0]
    cache_rows = window_cache.shape[1]
    cache_holders = window_cache.shape[0]
    stored_key_rows = window_cache[:, :, 0].reshape(cache_holders, cache_rows, heads_dev, head_dim)
    cache_values = window_cache[:, :, 1].reshape(cache_holders, cache_rows, heads_dev, head_dim)
    sink_count = sink_cache.shape[2]
    anchor_key_rows = sink_cache[0][:, :, 0].reshape(slot_count, sink_count, heads_dev, head_dim)
    sink_values = sink_cache[0][:, :, 1].reshape(slot_count, sink_count, heads_dev, head_dim)
    qkv_matrix = w_qkv[0].reshape(width, 3 * local_width)
    conv_weights = conv_taps[0]
    softmax_scale_factor = score_scale_table[0]
    gain_head = out_gain[0].reshape(heads_dev, head_dim)
    new_index = jnp.arange(token_count, dtype=jnp.int32)
    row_index = jnp.arange(cache_rows, dtype=jnp.int32)
    history = conv_history[0]
    new_keys = jnp.zeros((slot_count, token_count, heads_dev, head_dim), jnp.bfloat16)
    new_values = jnp.zeros((slot_count, token_count, heads_dev, head_dim), jnp.bfloat16)
    received = jnp.zeros((slot_count, width), jnp.bfloat16)
    produced = jnp.zeros((slot_count, token_count, width), jnp.bfloat16)
    for position in range(token_count + 1):
        t_raw = position - section_index
        is_valid = (t_raw >= 0) & (t_raw < token_count)
        t_index = jnp.clip(t_raw, 0, token_count - 1)
        fresh_input = embedded[:, min(position, token_count - 1)]
        stream_in = jnp.where(section_index == 0, fresh_input, received)
        mixer_history = history
        mixer_delta_state = delta_state
        mixer_new_keys = new_keys
        mixer_new_values = new_values
        normed = rms_scale(stream_in.astype(jnp.float32), pre_gain[0]).astype(jnp.bfloat16)
        projected = (
            jnp.dot(normed, qkv_matrix, preferred_element_type=jnp.float32)
            .astype(jnp.bfloat16)
            .reshape(slot_count, 3, local_width)
        )
        conv_window = jnp.concatenate([mixer_history, projected[:, None]], axis=1)
        activated = jax.nn.silu(
            jnp.sum(conv_window.astype(jnp.float32) * conv_weights[None], axis=1)
        )
        query_vec = unit_rows(activated[:, 0].reshape(slot_count, heads_dev, head_dim))
        key_vec = unit_rows(activated[:, 1].reshape(slot_count, heads_dev, head_dim))
        value_vec = activated[:, 2].reshape(slot_count, heads_dev, head_dim)
        beta_gate = jax.nn.sigmoid(jnp.dot(normed, w_beta[0], preferred_element_type=jnp.float32))
        predicted = jnp.einsum(
            "skhv,shk->shv", mixer_delta_state, key_vec, precision=lax.Precision.HIGHEST
        )
        update = jnp.transpose(key_vec, (0, 2, 1))[:, :, :, None] * (value_vec - predicted)[:, None]
        mixer_delta_state = mixer_delta_state + beta_gate[:, None, :, None] * update
        readout = jnp.einsum(
            "skhv,shk->shv", mixer_delta_state, query_vec, precision=lax.Precision.HIGHEST
        )
        query_halfwidth = query_vec.astype(jnp.bfloat16)
        mixer_new_keys = lax.dynamic_update_slice_in_dim(
            mixer_new_keys, key_vec.astype(jnp.bfloat16)[:, None], t_index, 1
        )
        mixer_new_values = lax.dynamic_update_slice_in_dim(
            mixer_new_values, value_vec.astype(jnp.bfloat16)[:, None], t_index, 1
        )
        anchor_score_rows = (
            jnp.einsum(
                "kry,kgry->krg",
                query_halfwidth,
                anchor_key_rows,
                preferred_element_type=jnp.float32,
            )
            * softmax_scale_factor[None, :, None]
        )
        incoming_score_rows = (
            jnp.einsum(
                "kry,kgry->krg", query_halfwidth, mixer_new_keys, preferred_element_type=jnp.float32
            )
            * softmax_scale_factor[None, :, None]
        )
        fresh_mask = (new_index <= t_index)[None, None, :]
        home_max = jnp.maximum(
            jnp.max(anchor_score_rows, axis=-1),
            jnp.max(jnp.where(fresh_mask, incoming_score_rows, negative_big), axis=-1),
        )
        limit = jnp.maximum(WIN - own_lengths, t_index + 1)
        cache_mask = row_index[None, None, :] >= limit[:, None, None]
        stored_score_rows = (
            jnp.einsum(
                "xqa,xeqa->xqe",
                query_halfwidth,
                stored_key_rows,
                preferred_element_type=jnp.float32,
            )
            * softmax_scale_factor[None, :, None]
        )
        highest = jnp.maximum(
            home_max, jnp.max(jnp.where(cache_mask, stored_score_rows, negative_big), axis=-1)
        )
        cache_weights = jnp.where(cache_mask, jnp.exp(stored_score_rows - highest[:, :, None]), 0.0)
        cache_sum = jnp.sum(cache_weights, axis=-1)
        cache_part = jnp.einsum(
            "shw,swhd->shd",
            cache_weights.astype(jnp.bfloat16),
            cache_values,
            preferred_element_type=jnp.float32,
        )
        sink_weights = jnp.exp(anchor_score_rows - highest[:, :, None])
        fresh_weights = jnp.where(
            fresh_mask, jnp.exp(incoming_score_rows - highest[:, :, None]), 0.0
        )
        weight_sum = cache_sum + jnp.sum(sink_weights, axis=-1) + jnp.sum(fresh_weights, axis=-1)
        numerator = cache_part + jnp.einsum(
            "shj,sjhd->shd",
            sink_weights.astype(jnp.bfloat16),
            sink_values,
            preferred_element_type=jnp.float32,
        )
        numerator = numerator + jnp.einsum(
            "shj,sjhd->shd",
            fresh_weights.astype(jnp.bfloat16),
            mixer_new_values,
            preferred_element_type=jnp.float32,
        )
        attended = numerator / weight_sum[:, :, None]
        mixed_heads = (
            (rms_scale(readout, gain_head[None]) + attended)
            .astype(jnp.bfloat16)
            .reshape(slot_count, local_width)
        )
        partial_out = jnp.dot(mixed_heads, w_out[0], preferred_element_type=jnp.float32)
        mixer_out = lax.psum(partial_out, "head")
        stream_out = (stream_in.astype(jnp.float32) + mixer_out).astype(jnp.bfloat16)
        mixer_history = jnp.concatenate([mixer_history[:, 1:], projected[:, None]], axis=1)
        stream_out, next_history, next_state, next_keys, next_values = (
            stream_out,
            mixer_history,
            mixer_delta_state,
            mixer_new_keys,
            mixer_new_values,
        )
        history = jnp.where(is_valid, next_history, history)
        delta_state = jnp.where(is_valid, next_state, delta_state)
        new_keys = jnp.where(is_valid, next_keys, new_keys)
        new_values = jnp.where(is_valid, next_values, new_values)
        stored = lax.dynamic_update_slice_in_dim(produced, stream_out[:, None], t_index, 1)
        produced = jnp.where(is_valid, stored, produced)
        if position < token_count:
            received = passed_along(stream_out, "section", 1)
    return (produced[None], delta_state[None])


def solution(mesh):
    return jax.shard_map(
        shards,
        mesh=mesh,
        in_specs=(
            P("req", None),
            P(),
            P(),
            P(("req", "head"), None),
            P("section", None, "req", None, "head"),
            P("section", None, "req", "head", None),
            P("section", "req", None, None, "head"),
            P("section", "req", None, None, "head"),
            P("section", None, None, "head"),
            P("section", "head", None),
            P("section", None, "head"),
            P("section", None, None, "head"),
            P("section", None),
            P("section", "head"),
            P("section", "head"),
        ),
        out_specs=(P("section", "req", None, None), P("section", "req", None, "head", None)),
        check_vma=False,
    )
```

profile of v0, /device:TPU:2, one launch (start us, length us, event | category | flops | bytes accessed | tf_op | source)
XLA Modules:
  0.0 1202.1 jit_solution(7097759639940147544)
XLA Ops:
  3.7 2.4 gather_fusion
  7.4 11.5 all-to-all-start
  18.9 66.6 %all-gather = s32[32,4,4]{2,1,0:T(4,128)S(1)} all-gather(s32[1,4,4]{2,1,0:T(4,128)S(1)} %bitcast.617), channel_id=1, replica_groups=mesh['section'=2,'req'=32,'head'=4] {'req'}, dimensions={0}, use_global_device_ids=true | all-gather | bytes 2112 | tf_op jit(solution)/shard_map/all_gather | solution.py:52
  85.6 4.1 fusion.75
  89.7 3.2 copy.413
  92.9 5.1 gather_fusion.2
  98.0 4.7 fusion
  103.7 8.2 all-to-all-start.1
  111.9 792.8 %all-reduce.1 = bf16[512,2048]{1,0:T(8,128)(2,1)} all-reduce(f32[512,2048]{1,0:T(8,128)} %fusion.75), channel_id=1, replica_groups=mesh['section'=2,'req'=32,'head'=4] {'req','head'}, use_global_device_ids=true, to_apply=%region_0.0 | all-reduce | flops 1048576 | bytes 6291456 | tf_op jit(solution)/shard_map/psum | solution.py:58
  905.6 8.8 copy.140
  915.4 4.5 convolution_convert_fusion.4
  929.7 2.7 copy.144
  932.4 2.5 fusion.279
  934.9 4.2 copy.145
  939.1 2.0 fusion.214
  941.5 4.2 copy.146
  945.8 2.2 fusion.114
  948.7 20.5 %psum.43 = f32[4,2048]{1,0:T(4,128)S(1)} all-reduce(f32[4,2048]{1,0:T(4,128)S(1)} %fusion.9), channel_id=1, replica_groups=mesh['section'=2,'req'=32,'head'=4] {'head'}, use_global_device_ids=true, to_apply=%region_12.13 | all-reduce | flops 8192 | bytes 65536 | tf_op jit(solution)/shard_map/psum | solution.py:192
  969.9 2.0 collective-permute-start
  978.5 4.5 convolution_convert_fusion.3
  988.2 2.0 fusion.210
  992.0 1.9 convert_bitcast_fusion.4
  994.0 1.9 fusion.188
  997.7 2.1 fusion.42
  1000.6 2.1 fusion.35
  1005.6 15.6 %psum.44 = f32[4,2048]{1,0:T(4,128)} all-reduce(f32[4,2048]{1,0:T(4,128)} %fusion.7), channel_id=1, replica_groups=mesh['section'=2,'req'=32,'head'=4] {'head'}, use_global_device_ids=true, to_apply=%region_24.25 | all-reduce | flops 8192 | bytes 65536 | tf_op jit(solution)/shard_map/psum | solution.py:192
  1023.2 1.9 collective-permute-start.1
  1033.1 4.5 convolution_convert_fusion.2
  1044.1 2.0 fusion.206
  1050.8 1.9 fusion.190
  1055.3 2.2 fusion.271
  1057.8 2.7 fusion.33
  1062.5 16.8 %psum.45 = f32[4,2048]{1,0:T(4,128)} all-reduce(f32[4,2048]{1,0:T(4,128)S(1)} %fusion.5), channel_id=1, replica_groups=mesh['section'=2,'req'=32,'head'=4] {'head'}, use_global_device_ids=true, to_apply=%region_36.37 | all-reduce | flops 8192 | bytes 65536 | tf_op jit(solution)/shard_map/psum | solution.py:192
  1081.5 2.1 collective-permute-start.2
  1092.9 4.5 convolution_convert_fusion.1
  1101.9 2.0 fusion.202
  1107.1 1.9 convert_bitcast_fusion.2
  1109.0 1.9 fusion.192
  1112.9 2.5 fusion.80
  1115.6 3.4 fusion.31
  1121.9 15.6 %psum.46 = f32[4,2048]{1,0:T(4,128)} all-reduce(f32[4,2048]{1,0:T(4,128)} %fusion.3), channel_id=1, replica_groups=mesh['section'=2,'req'=32,'head'=4] {'head'}, use_global_device_ids=true, to_apply=%region_48.49 | all-reduce | flops 8192 | bytes 65536 | tf_op jit(solution)/shard_map/psum | solution.py:192
  1139.0 1.9 collective-permute-start.3
  1146.6 4.5 convolution_convert_fusion
  1156.2 2.0 fusion.198
  1166.7 3.6 fusion.39
  1172.0 3.4 fusion.26
  1177.1 16.8 %psum.47 = f32[4,2048]{1,0:T(4,128)} all-reduce(f32[4,2048]{1,0:T(4,128)S(1)} %fusion.1), channel_id=1, replica_groups=mesh['section'=2,'req'=32,'head'=4] {'head'}, use_global_device_ids=true, to_apply=%region_60.61 | all-reduce | flops 8192 | bytes 65536 | tf_op jit(solution)/shard_map/psum | solution.py:192
  1196.8 5.1 add_select_fusion
  (491 shorter events, 114.1 us)
Async XLA Ops:
  0.6 947.7 %copy-start = (bf16[1,512,2048]{2,1,0:T(8,128)(2,1)S(1)}, bf16[1,512,2048]{2,1,0:T(8,128)(2,1)}, u32[]{:S(2)}) copy-start(bf16[1,512,2048]{2,1,0:T(8,128)(2,1)} %param.24) | copy-start | bytes 6291460
  6.1 12.8 %copy-start.117 = (s32[4,4]{1,0:T(4,128)S(1)}, s32[4,4]{1,0:T(4,128)}, u32[]{:S(2)}) copy-start(s32[4,4]{1,0:T(4,128)} %param.15) | copy-start | bytes 196
  7.4 95.3 %all-to-all-start = ((f32[1,128,4,4,128]{4,3,2,0,1:T(4,128)}), f32[1,128,4,4,128]{4,3,2,0,1:T(4,128)S(1)}, u32[]{:S(2)}, u32[]{:S(2)}) async-start(f32[1,128,4,4,128]{4,3,2,0,1:T(4,128)} %bitcast_select_fusion.1), calls=%async_computation | async-start | bytes 2097152 | tf_op jit(solution)/shard_map/all_to_all | solution.py:64
  103.7 826.0 %all-to-all-start.1 = ((bf16[1,128,16,2,512]{4,2,3,0,1:T(8,128)(2,1)}), bf16[1,128,16,2,512]{4,2,3,0,1:T(8,128)(2,1)}, u32[]{:S(2)}, u32[]{:S(2)}) async-start(bf16[1,128,16,2,512]{4,2,3,0,1:T(8,128)(2,1)} %fusion), calls=%async_computation.1 | async-start | bytes 8388608 | tf_op jit(solution)/shard_map/all_to_all | solution.py:68
  111.8 792.8 %copy-start.11 = (bf16[1,4,3,3,512]{4,1,3,2,0:T(4,128)(2,1)S(1)}, bf16[1,4,3,3,512]{4,1,3,2,0:T(4,128)(2,1)}, u32[]{:S(2)}) copy-start(bf16[1,4,3,3,512]{4,1,3,2,0:T(4,128)(2,1)} %param.21) | copy-start | bytes 110596
  111.8 792.8 %copy-start.80 = (f32[1,4,3,512]{3,1,2,0:T(4,128)S(1)}, f32[1,4,3,512]{3,1,2,0:T(4,128)}, u32[]{:S(2)}) copy-start(f32[1,4,3,512]{3,1,2,0:T(4,128)} %param.26) | copy-start | bytes 73732
  905.6 9.7 copy-start.12
  915.3 6.7 copy-start.22
  915.3 7.3 copy-start.13
  915.3 9.7 copy-start.118
  922.2 7.4 copy-start.92
  922.2 25.9 %copy-start.87 = (bf16[4,4,512]{2,1,0:T(4,128)(2,1)}, bf16[4,4,512]{2,1,0:T(4,128)(2,1)S(1)}, u32[]{:S(2)}) copy-start(bf16[4,4,512]{2,1,0:T(4,128)(2,1)S(1)} %get-tuple-element.16) | copy-start | bytes 49156
  924.9 4.7 copy-start.34
  925.9 57.2 %copy-start.8 = (bf16[4,3,3,512]{3,0,2,1:T(4,128)(2,1)}, bf16[4,3,3,512]{3,0,2,1:T(4,128)(2,1)S(1)}, u32[]{:S(2)}) copy-start(bf16[4,3,3,512]{3,0,2,1:T(4,128)(2,1)S(1)} %maximum_select_fusion) | copy-start | bytes 110596
  969.9 7.7 collective-permute-start
  977.7 5.3 copy-start.16
  984.3 16.2 %copy-start.30 = (f32[4,4,128]{2,1,0:T(4,128)S(1)}, f32[4,4,128]{2,1,0:T(4,128)}, u32[]{:S(2)}) copy-start(f32[4,4,128]{2,1,0:T(4,128)} %copy-done.29) | copy-start | bytes 24580
  984.3 16.2 %copy-start.35 = (f32[4,128,4]{1,2,0:T(4,128)S(1)}, f32[4,128,4]{1,2,0:T(4,128)}, u32[]{:S(2)}) copy-start(f32[4,128,4]{1,2,0:T(4,128)} %copy-done.34) | copy-start | bytes 24580
  985.1 17.6 %copy-start.64 = (f32[4,128,4]{1,2,0:T(4,128)}, f32[4,128,4]{1,2,0:T(4,128)S(1)}, u32[]{:S(2)}) copy-start(f32[4,128,4]{1,2,0:T(4,128)S(1)} %fusion.317) | copy-start | bytes 24580
  987.3 9.8 copy-start.79
  997.7 5.1 copy-start.1
  997.7 5.2 copy-start.14
  1002.9 18.3 %slice-start = ((bf16[4,3,3,512]{3,0,2,1:T(4,128)(2,1)}), bf16[4,2,3,512]{3,0,2,1:T(4,128)(2,1)S(1)}, s32[]{:S(2)}) async-start(bf16[4,3,3,512]{3,0,2,1:T(4,128)(2,1)} %copy-done.8), calls=%async_computation.2 | async-start | bytes 49152 | tf_op jit(solution)/shard_map/slice | solution.py:194
  1002.9 18.3 %copy-start.25 = (bf16[4,1536]{1,0:T(4,128)(2,1)S(1)}, bf16[4,1536]{1,0:T(4,128)(2,1)}, u32[]{:S(2)}) copy-start(bf16[4,1536]{1,0:T(4,128)(2,1)} %copy-done.24) | copy-start | bytes 36868
  1023.2 7.5 collective-permute-start.1
  1025.8 4.9 copy-start.20
  1026.6 11.1 copy-start.21
  1031.6 6.0 copy-start.17
  1033.1 4.5 copy-start.10
  1037.7 17.7 %copy-start.31 = (f32[4,4,128]{2,1,0:T(4,128)S(1)}, f32[4,4,128]{2,1,0:T(4,128)}, u32[]{:S(2)}) copy-start(f32[4,4,128]{2,1,0:T(4,128)} %copy-done.29) | copy-start | bytes 24580
  1046.1 11.5 copy-start.36
  1080.1 17.3 %copy-start.9 = (bf16[4,3,3,512]{3,0,2,1:T(4,128)(2,1)}, bf16[4,3,3,512]{3,0,2,1:T(4,128)(2,1)S(1)}, u32[]{:S(2)}) copy-start(bf16[4,3,3,512]{3,0,2,1:T(4,128)(2,1)S(1)} %maximum_select_fusion.2) | copy-start | bytes 110596
  1081.5 8.9 collective-permute-start.2
  1091.3 6.0 copy-start.18
  1119.2 18.3 %slice-start.1 = ((bf16[4,3,3,512]{3,0,2,1:T(4,128)(2,1)}), bf16[4,2,3,512]{3,0,2,1:T(4,128)(2,1)S(1)}, s32[]{:S(2)}) async-start(bf16[4,3,3,512]{3,0,2,1:T(4,128)(2,1)} %copy-done.9), calls=%async_computation.3 | async-start | bytes 49152 | tf_op jit(solution)/shard_map/slice | solution.py:194
  1119.2 18.3 %copy-start.27 = (bf16[4,1536]{1,0:T(4,128)(2,1)S(1)}, bf16[4,1536]{1,0:T(4,128)(2,1)}, u32[]{:S(2)}) copy-start(bf16[4,1536]{1,0:T(4,128)(2,1)} %copy-done.26) | copy-start | bytes 36868
  1139.0 6.7 collective-permute-start.3
  1146.6 5.4 copy-start.19
  1151.1 9.4 copy-start.81
  1156.2 9.9 copy-start.78
  1166.7 5.3 copy-start.33
  1166.7 5.3 copy-start.38
  1166.7 5.3 copy-start.55
  1166.7 5.3 copy-start.58
  1166.7 5.3 copy-start.61
  1175.7 21.1 %copy-start.5 = (f32[1,4,32,4,4,128]{5,4,3,2,1,0:T(4,128)S(1)}, f32[1,4,32,4,4,128]{5,4,3,2,1,0:T(4,128)}, u32[]{:S(2)}) copy-start(f32[1,4,32,4,4,128]{5,4,3,2,1,0:T(4,128)} %copy.150) | copy-start | bytes 3145732
  1176.4 20.4 %copy-start.59 = (f32[4,4,128]{2,1,0:T(4,128)S(1)}, f32[4,4,128]{2,1,0:T(4,128)}, u32[]{:S(2)}) copy-start(f32[4,4,128]{2,1,0:T(4,128)} %copy-done.56) | copy-start | bytes 24580
  1176.4 20.4 %copy-start.62 = (f32[4,4,128]{2,1,0:T(4,128)S(1)}, f32[4,4,128]{2,1,0:T(4,128)}, u32[]{:S(2)}) copy-start(f32[4,4,128]{2,1,0:T(4,128)} %copy-done.60) | copy-start | bytes 24580
  (81 other events, 219.1 us)
where the time goes:
time: 1210 us; the launch traced here: 1200 us
  blocking collectives  945 us (78%)
  matrix products  81.3 us (7%)
  local copies, waits for them, and re-layouts  76.8 us (6%)
  other arithmetic  69.3 us (6%)
  starting transfers between devices  27.5 us (2%)
    psum x1, blocking collectives, shards(): summed = lax.psum(looked_up, ('req', 'head'))  793 us
    psum x5, blocking collectives, shards(): mixer_out = lax.psum(partial_out, 'head')  85.3 us
    all_gather x1, blocking collectives, shards(): all_ids = lax.all_gather(token_ids, 'req', axis=0, tiled=True)  66.6 us
  transfers between devices with their start and end apart: 6, of which 0 were waited for; matrix products, arithmetic and copies ran while one was open for 5% of the time, Pallas kernels for 0%

commit v1 on v0

--- a/solution.py
+++ b/solution.py
@@ -2,6 +2,7 @@
 import jax.numpy as jnp
 from jax import lax
 from jax.sharding import PartitionSpec as P
+from jax.lax import psum
 
 WIN = 512
 epsilon = 1e-06
@@ -41,6 +42,12 @@
     out_gain,
     score_scale_table,
 ):
+
+    def seats_all_trace(my_tile):
+        for ii in ("head", "req"):
+            my_tile = psum(my_tile, ii)
+        return my_tile
+
     slot_count, token_count = token_ids.shape
     heads_dev = score_scale_table.shape[1]
     width = pre_gain.shape[1]
@@ -55,7 +62,7 @@
         all_ids.reshape(-1)[:, None] == first_row + jnp.arange(vocab_dev, dtype=jnp.int32)[None, :]
     ).astype(jnp.bfloat16)
     looked_up = jnp.dot(onehot, embed_table, preferred_element_type=jnp.float32)
-    summed = lax.psum(looked_up, ("req", "head"))
+    summed = seats_all_trace(looked_up)
     own_rows = lax.dynamic_slice_in_dim(
         summed, group_index * slot_count * token_count, slot_count * token_count, 0
     )

time: 1210 us -> 645 us (0.53)
  blocking collectives: 945 us -> 324 us
  waiting for transfers between devices: 0.02 us -> 41 us
  between operations: 2.47 us -> 15.8 us
    psum x1, blocking collectives: 793 us -> 193 us  [seats_all_trace(): my_tile = psum(my_tile, ii)]
    psum x0 -> x1, waiting for transfers between devices: none -> 40.3 us  [seats_all_trace(): my_tile = psum(my_tile, ii)]
    all_gather x1, blocking collectives: 66.6 us -> 52.3 us  [shards(): all_ids = lax.all_gather(token_ids, 'req', axis=0, tiled=True)]
    unnamed x252 -> x248, local copies, waits for them, and re-layouts: 23.8 us -> 26.5 us
  transfers between devices with their start and end apart: 6 -> 7, of which waited for: 0 -> 2; matrix products, arithmetic and copies ran while one was open for 5% -> 11% of each run, Pallas kernels for 0% -> 0%
where the time goes in v1:
time: 645 us; the launch traced here: 634 us
  blocking collectives  324 us (50%)
  matrix products  82 us (13%)
  local copies, waits for them, and re-layouts  79.2 us (12%)
  other arithmetic  68.4 us (11%)
  waiting for transfers between devices  41 us (6%)
  starting transfers between devices  23.3 us (4%)
  between operations  15.8 us (2%)
    psum x1, blocking collectives, seats_all_trace(): my_tile = psum(my_tile, ii)  193 us
    psum x5, blocking collectives, shards(): mixer_out = lax.psum(partial_out, 'head')  78.8 us
    all_gather x1, blocking collectives, shards(): all_ids = lax.all_gather(token_ids, 'req', axis=0, tiled=True)  52.3 us
    psum x1, waiting for transfers between devices, seats_all_trace(): my_tile = psum(my_tile, ii)  40.3 us
    unnamed x248, local copies, waits for them, and re-layouts  26.5 us
    dot_general x5, matrix products, shards(): jnp.dot(normed, qkv_matrix, preferred_element_type=jnp.float32)  22.5 us
    dot_general x5, matrix products, shards(): jnp.einsum('skhv,shk->shv', mixer_delta_state, query_vec, precision=lax.P...  12.9 us
  transfers between devices with their start and end apart: 7, of which 2 were waited for; matrix products, arithmetic and copies ran while one was open for 11% of the time, Pallas kernels for 0%

profile of v1, /device:TPU:2, one launch (start us, length us, event | category | flops | bytes accessed | tf_op | source)
XLA Modules:
  0.0 633.7 jit_solution(8546508393771573547)
XLA Ops:
  7.2 52.3 %all-gather = s32[32,4,4]{2,1,0:T(4,128)S(1)} all-gather(s32[1,4,4]{2,1,0:T(4,128)} %bitcast.617), channel_id=1, replica_groups=mesh['section'=2,'req'=32,'head'=4] {'req'}, dimensions={0}, use_global_device_ids=true | all-gather | bytes 2112 | tf_op jit(solution)/shard_map/all_gather | solution.py:59
  59.6 4.1 fusion.75
  65.6 2.4 gather_fusion
  69.3 6.1 all-to-all-start
  75.5 5.3 copy.413
  80.8 5.1 gather_fusion.2
  88.4 4.7 fusion
  94.7 9.3 %all-to-all-start.1 = ((bf16[1,128,16,2,512]{4,2,3,0,1:T(8,128)(2,1)}), bf16[1,128,16,2,512]{4,2,3,0,1:T(8,128)(2,1)}, u32[]{:S(2)}, u32[]{:S(2)}) async-start(bf16[1,128,16,2,512]{4,2,3,0,1:T(8,128)(2,1)} %fusion), calls=%async_computation.1 | async-start | bytes 8388608 | tf_op jit(solution)/shard_map/all_to_all | solution.py:75
  104.6 8.9 %copy.140 = bf16[1,2048,3,512]{1,3,2,0:T(8,128)(2,1)} copy(bf16[1,2048,3,512]{3,1,2,0:T(8,128)(2,1)} %param.23) | data formatting | bytes 12582912 | tf_op args[8]
  117.9 40.3 %all-reduce.3.cloned.1.call-done = f32[512,2048]{1,0:T(8,128)} async-done(((f32[512,2048]{1,0:T(8,128)}), f32[512,2048]{1,0:T(8,128)}) %all-reduce.3.cloned.1.call-update) | async-done | bytes 4194320 | tf_op jit(solution)/shard_map/psum | solution.py:48
  158.3 193.1 %all-reduce.4 = bf16[512,2048]{1,0:T(8,128)(2,1)} all-reduce(f32[512,2048]{1,0:T(8,128)} %all-reduce.3.cloned.1.call-done), channel_id=1, replica_groups=mesh['section'=2,'req'=32,'head'=4] {'req'}, use_global_device_ids=true, to_apply=%region_1.0 | all-reduce | flops 1048576 | bytes 6291456 | tf_op jit(solution)/shard_map/psum | solution.py:48
  353.1 4.5 convolution_convert_fusion.4
  361.4 2.7 copy.144
  364.1 2.5 fusion.279
  366.5 4.2 copy.145
  370.7 2.0 fusion.214
  373.2 4.2 copy.146
  377.5 2.2 fusion.114
  380.4 13.6 %psum.51 = f32[4,2048]{1,0:T(4,128)S(1)} all-reduce(f32[4,2048]{1,0:T(4,128)S(1)} %fusion.9), channel_id=1, replica_groups=mesh['section'=2,'req'=32,'head'=4] {'head'}, use_global_device_ids=true, to_apply=%region_13.14 | all-reduce | flops 8192 | bytes 65536 | tf_op jit(solution)/shard_map/psum | solution.py:199
  394.6 2.0 collective-permute-start
  403.2 4.5 convolution_convert_fusion.3
  412.8 2.0 fusion.210
  416.6 1.9 convert_bitcast_fusion.4
  422.2 2.1 fusion.42
  425.1 2.1 fusion.35
  430.1 17.8 %psum.52 = f32[4,2048]{1,0:T(4,128)} all-reduce(f32[4,2048]{1,0:T(4,128)} %fusion.7), channel_id=1, replica_groups=mesh['section'=2,'req'=32,'head'=4] {'head'}, use_global_device_ids=true, to_apply=%region_25.26 | all-reduce | flops 8192 | bytes 65536 | tf_op jit(solution)/shard_map/psum | solution.py:199
  459.8 4.5 convolution_convert_fusion.2
  470.8 2.0 fusion.206
  477.3 1.9 fusion.190
  481.8 2.2 fusion.271
  484.3 2.7 fusion.33
  489.0 14.9 %psum.53 = f32[4,2048]{1,0:T(4,128)} all-reduce(f32[4,2048]{1,0:T(4,128)S(1)} %fusion.5), channel_id=1, replica_groups=mesh['section'=2,'req'=32,'head'=4] {'head'}, use_global_device_ids=true, to_apply=%region_37.38 | all-reduce | flops 8192 | bytes 65536 | tf_op jit(solution)/shard_map/psum | solution.py:199
  506.1 2.1 collective-permute-start.2
  517.5 4.5 convolution_convert_fusion.1
  526.6 2.0 fusion.202
  531.7 1.9 convert_bitcast_fusion.2
  533.7 1.9 fusion.192
  537.6 2.5 fusion.80
  540.3 3.4 fusion.31
  546.6 17.5 %psum.54 = f32[4,2048]{1,0:T(4,128)} all-reduce(f32[4,2048]{1,0:T(4,128)} %fusion.3), channel_id=1, replica_groups=mesh['section'=2,'req'=32,'head'=4] {'head'}, use_global_device_ids=true, to_apply=%region_49.50 | all-reduce | flops 8192 | bytes 65536 | tf_op jit(solution)/shard_map/psum | solution.py:199
  565.6 1.9 collective-permute-start.3
  573.2 4.5 convolution_convert_fusion
  582.8 2.0 fusion.198
  589.5 1.9 fusion.194
  593.3 3.6 fusion.39
  598.6 3.4 fusion.26
  603.7 14.9 %psum.55 = f32[4,2048]{1,0:T(4,128)} all-reduce(f32[4,2048]{1,0:T(4,128)S(1)} %fusion.1), channel_id=1, replica_groups=mesh['section'=2,'req'=32,'head'=4] {'head'}, use_global_device_ids=true, to_apply=%region_61.62 | all-reduce | flops 8192 | bytes 65536 | tf_op jit(solution)/shard_map/psum | solution.py:199
  621.6 5.1 add_select_fusion
  (490 shorter events, 116.6 us)
Async XLA Ops:
  7.2 372.8 %copy-start = (bf16[1,512,2048]{2,1,0:T(8,128)(2,1)S(1)}, bf16[1,512,2048]{2,1,0:T(8,128)(2,1)}, u32[]{:S(2)}) copy-start(bf16[1,512,2048]{2,1,0:T(8,128)(2,1)} %param.24) | copy-start | bytes 6291460
  7.2 151.1 %all-reduce.3.cloned.1.call-start = ((), (), s32[]{:S(2)}) async-start(), calls=%async_computation.2 | async-start | bytes 8388608 | tf_op jit(solution)/shard_map/psum | solution.py:48
  69.3 24.5 %all-to-all-start = ((f32[1,128,4,4,128]{4,3,2,0,1:T(4,128)}), f32[1,128,4,4,128]{4,3,2,0,1:T(4,128)S(1)}, u32[]{:S(2)}, u32[]{:S(2)}) async-start(f32[1,128,4,4,128]{4,3,2,0,1:T(4,128)} %bitcast_select_fusion.1), calls=%async_computation | async-start | bytes 2097152 | tf_op jit(solution)/shard_map/all_to_all | solution.py:71
  80.8 6.8 %copy-start.22 = (bf16[1,4,4,2,512]{4,3,2,1,0:T(2,128)(2,1)S(1)}, bf16[1,4,4,2,512]{4,3,2,1,0:T(2,128)(2,1)}, u32[]{:S(2)}) copy-start(bf16[1,4,4,2,512]{4,3,2,1,0:T(2,128)(2,1)} %param.22) | copy-start | bytes 98308
  87.7 273.1 %copy-start.91 = (bf16[4,4,512]{2,1,0:T(4,128)(2,1)}, bf16[4,4,512]{2,1,0:T(4,128)(2,1)S(1)}, u32[]{:S(2)}) copy-start(bf16[4,4,512]{2,1,0:T(4,128)(2,1)S(1)} %get-tuple-element.17) | copy-start | bytes 49156
  87.7 292.0 %copy-start.86 = (bf16[4,4,512]{2,1,0:T(4,128)(2,1)}, bf16[4,4,512]{2,1,0:T(4,128)(2,1)S(1)}, u32[]{:S(2)}) copy-start(bf16[4,4,512]{2,1,0:T(4,128)(2,1)S(1)} %get-tuple-element.16) | copy-start | bytes 49156
  93.1 11.4 %copy-start.11 = (bf16[1,4,3,3,512]{4,1,3,2,0:T(4,128)(2,1)S(1)}, bf16[1,4,3,3,512]{4,1,3,2,0:T(4,128)(2,1)}, u32[]{:S(2)}) copy-start(bf16[1,4,3,3,512]{4,1,3,2,0:T(4,128)(2,1)} %param.21) | copy-start | bytes 110596
  93.1 11.4 %copy-start.79 = (f32[1,4,3,512]{3,1,2,0:T(4,128)S(1)}, f32[1,4,3,512]{3,1,2,0:T(4,128)}, u32[]{:S(2)}) copy-start(f32[1,4,3,512]{3,1,2,0:T(4,128)} %param.26) | copy-start | bytes 73732
  94.7 266.6 %all-to-all-start.1 = ((bf16[1,128,16,2,512]{4,2,3,0,1:T(8,128)(2,1)}), bf16[1,128,16,2,512]{4,2,3,0,1:T(8,128)(2,1)}, u32[]{:S(2)}, u32[]{:S(2)}) async-start(bf16[1,128,16,2,512]{4,2,3,0,1:T(8,128)(2,1)} %fusion), calls=%async_computation.1 | async-start | bytes 8388608 | tf_op jit(solution)/shard_map/all_to_all | solution.py:75
  117.9 235.2 %copy-start.12 = (f32[1,2048]{1,0:T(1,128)S(1)}, f32[1,2048]{1,0:T(1,128)}, u32[]{:S(2)}) copy-start(f32[1,2048]{1,0:T(1,128)} %param.27) | copy-start | bytes 24580
  353.1 6.2 copy-start.117
  359.0 5.1 copy-start.28
  359.2 4.8 copy-start.33
  361.3 46.4 %copy-start.8 = (bf16[4,3,3,512]{3,0,2,1:T(4,128)(2,1)}, bf16[4,3,3,512]{3,0,2,1:T(4,128)(2,1)S(1)}, u32[]{:S(2)}) copy-start(bf16[4,3,3,512]{3,0,2,1:T(4,128)(2,1)S(1)} %maximum_select_fusion) | copy-start | bytes 110596
  394.6 6.2 collective-permute-start
  401.7 6.0 copy-start.16
  409.0 16.0 %copy-start.29 = (f32[4,4,128]{2,1,0:T(4,128)S(1)}, f32[4,4,128]{2,1,0:T(4,128)}, u32[]{:S(2)}) copy-start(f32[4,4,128]{2,1,0:T(4,128)} %copy-done.28) | copy-start | bytes 24580
  409.0 16.0 %copy-start.34 = (f32[4,128,4]{1,2,0:T(4,128)S(1)}, f32[4,128,4]{1,2,0:T(4,128)}, u32[]{:S(2)}) copy-start(f32[4,128,4]{1,2,0:T(4,128)} %copy-done.33) | copy-start | bytes 24580
  409.8 17.5 %copy-start.63 = (f32[4,128,4]{1,2,0:T(4,128)}, f32[4,128,4]{1,2,0:T(4,128)S(1)}, u32[]{:S(2)}) copy-start(f32[4,128,4]{1,2,0:T(4,128)S(1)} %fusion.317) | copy-start | bytes 24580
  411.9 9.7 %copy-start.78 = (f32[4,1,512]{2,0,1:T(4,128)S(1)}, f32[4,1,512]{2,0,1:T(4,128)}, u32[]{:S(2)}) copy-start(f32[4,1,512]{2,0,1:T(4,128)} %get-tuple-element.97) | copy-start | bytes 24580
  422.2 5.1 copy-start.2
  422.2 5.2 copy-start.14
  427.4 20.5 %slice-start = ((bf16[4,3,3,512]{3,0,2,1:T(4,128)(2,1)}), bf16[4,2,3,512]{3,0,2,1:T(4,128)(2,1)S(1)}, s32[]{:S(2)}) async-start(bf16[4,3,3,512]{3,0,2,1:T(4,128)(2,1)} %copy-done.8), calls=%async_computation.3 | async-start | bytes 49152 | tf_op jit(solution)/shard_map/slice | solution.py:201
  427.4 20.5 %copy-start.24 = (bf16[4,1536]{1,0:T(4,128)(2,1)S(1)}, bf16[4,1536]{1,0:T(4,128)(2,1)}, u32[]{:S(2)}) copy-start(bf16[4,1536]{1,0:T(4,128)(2,1)} %copy-done.23) | copy-start | bytes 36868
  449.9 7.5 %collective-permute-start.1 = (bf16[4,2048]{1,0:T(4,128)(2,1)}, bf16[4,2048]{1,0:T(4,128)(2,1)}, u32[]{:S(2)}, u32[]{:S(2)}) collective-permute-start(bf16[4,2048]{1,0:T(4,128)(2,1)} %get-tuple-element.57), channel_id=1, source_target_pairs={{0,128},{1,129},{2,130},{3,131},{4,132},{5,133},{6,134},{7,135},{8... | collective-permute-start | bytes 49160 | tf_op jit(solution)/shard_map/ppermute | solution.py:15
  452.5 4.9 copy-start.20
  453.2 11.1 %copy-start.21 = (bf16[2,4,8,128]{3,2,0,1:T(8,128)(2,1)}, bf16[2,4,8,128]{3,2,0,1:T(8,128)(2,1)S(1)}, u32[]{:S(2)}) copy-start(bf16[2,4,8,128]{3,2,0,1:T(8,128)(2,1)S(1)} %broadcast_select_fusion.5) | copy-start | bytes 49156
  458.3 6.0 copy-start.17
  459.8 4.5 copy-start.10
  464.3 17.5 %copy-start.30 = (f32[4,4,128]{2,1,0:T(4,128)S(1)}, f32[4,4,128]{2,1,0:T(4,128)}, u32[]{:S(2)}) copy-start(f32[4,4,128]{2,1,0:T(4,128)} %copy-done.28) | copy-start | bytes 24580
  472.8 11.3 %copy-start.35 = (f32[4,128,4]{1,2,0:T(4,128)S(1)}, f32[4,128,4]{1,2,0:T(4,128)}, u32[]{:S(2)}) copy-start(f32[4,128,4]{1,2,0:T(4,128)} %copy-done.33) | copy-start | bytes 24580
  504.7 17.3 %copy-start.9 = (bf16[4,3,3,512]{3,0,2,1:T(4,128)(2,1)}, bf16[4,3,3,512]{3,0,2,1:T(4,128)(2,1)S(1)}, u32[]{:S(2)}) copy-start(bf16[4,3,3,512]{3,0,2,1:T(4,128)(2,1)S(1)} %maximum_select_fusion.2) | copy-start | bytes 110596
  506.1 8.9 %collective-permute-start.2 = (bf16[4,2048]{1,0:T(4,128)(2,1)}, bf16[4,2048]{1,0:T(4,128)(2,1)}, u32[]{:S(2)}, u32[]{:S(2)}) collective-permute-start(bf16[4,2048]{1,0:T(4,128)(2,1)} %get-tuple-element.51), channel_id=1, source_target_pairs={{0,128},{1,129},{2,130},{3,131},{4,132},{5,133},{6,134},{7,135},{8... | collective-permute-start | bytes 49160 | tf_op jit(solution)/shard_map/ppermute | solution.py:15
  516.0 6.0 copy-start.18
  543.9 20.2 %slice-start.1 = ((bf16[4,3,3,512]{3,0,2,1:T(4,128)(2,1)}), bf16[4,2,3,512]{3,0,2,1:T(4,128)(2,1)S(1)}, s32[]{:S(2)}) async-start(bf16[4,3,3,512]{3,0,2,1:T(4,128)(2,1)} %copy-done.9), calls=%async_computation.4 | async-start | bytes 49152 | tf_op jit(solution)/shard_map/slice | solution.py:201
  543.9 20.2 %copy-start.26 = (bf16[4,1536]{1,0:T(4,128)(2,1)S(1)}, bf16[4,1536]{1,0:T(4,128)(2,1)}, u32[]{:S(2)}) copy-start(bf16[4,1536]{1,0:T(4,128)(2,1)} %copy-done.25) | copy-start | bytes 36868
  565.6 6.7 %collective-permute-start.3 = (bf16[4,2048]{1,0:T(4,128)(2,1)S(1)}, bf16[4,2048]{1,0:T(4,128)(2,1)}, u32[]{:S(2)}, u32[]{:S(2)}) collective-permute-start(bf16[4,2048]{1,0:T(4,128)(2,1)S(1)} %get-tuple-element.45), channel_id=1, source_target_pairs={{0,128},{1,129},{2,130},{3,131},{4,132},{5,133},{6,134},{7,135},{8... | collective-permute-start | bytes 49160 | tf_op jit(solution)/shard_map/ppermute | solution.py:15
  573.2 5.4 copy-start.19
  577.7 9.4 %copy-start.80 = (pred[4,512]{1,0:T(4,128)(4,1)S(1)}, pred[4,512]{1,0:T(4,128)(4,1)}, u32[]{:S(2)}) copy-start(pred[4,512]{1,0:T(4,128)(4,1)} %iota_compare_fusion) | copy-start | bytes 6148
  582.8 9.9 %copy-start.77 = (f32[4,1,512]{2,0,1:T(4,128)S(1)}, f32[4,1,512]{2,0,1:T(4,128)}, u32[]{:S(2)}) copy-start(f32[4,1,512]{2,0,1:T(4,128)} %get-tuple-element.88) | copy-start | bytes 24580
  593.3 5.3 copy-start.32
  593.3 5.3 copy-start.37
  593.3 5.3 copy-start.54
  593.3 5.3 copy-start.57
  593.3 5.3 copy-start.60
  602.4 19.2 %copy-start.6 = (f32[1,4,32,4,4,128]{5,4,3,2,1,0:T(4,128)S(1)}, f32[1,4,32,4,4,128]{5,4,3,2,1,0:T(4,128)}, u32[]{:S(2)}) copy-start(f32[1,4,32,4,4,128]{5,4,3,2,1,0:T(4,128)} %copy.150) | copy-start | bytes 3145732
  603.0 18.5 %copy-start.58 = (f32[4,4,128]{2,1,0:T(4,128)S(1)}, f32[4,4,128]{2,1,0:T(4,128)}, u32[]{:S(2)}) copy-start(f32[4,4,128]{2,1,0:T(4,128)} %copy-done.55) | copy-start | bytes 24580
  603.0 18.5 %copy-start.61 = (f32[4,4,128]{2,1,0:T(4,128)S(1)}, f32[4,4,128]{2,1,0:T(4,128)}, u32[]{:S(2)}) copy-start(f32[4,4,128]{2,1,0:T(4,128)} %copy-done.59) | copy-start | bytes 24580
  (80 other events, 209.2 us)
Sparse Core Ops, SparseCore 0:
  63.8 94.3 all-reduce.2
